TPU v7x, 512 devices: a whole 4x4x16 slice. The times are simulated.
512 devices in a mesh: seq: 32 (over z, core), tensor: 16 (over y, x).
Axes of the slice: x: 4, y: 4, z: 16, core: 2. Of those that a mesh axis runs over, the one named last changes fastest.
Arguments:
- hidden: bfloat16 [4, 64, 5120], P(None, None, 'seq'), may hold values from -400 to 400
- norm_gain: bfloat16 [5120], P('seq'), may hold values from 0.099609375 to 1.8984375
- w_qkv: bfloat16 [5120, 7168], P('seq', 'tensor'), may hold values from -0.078125 to 0.078125
- b_qkv: bfloat16 [7168], P('tensor'), may hold values from -3 to 3
- w_out: bfloat16 [5120, 5120], P('tensor', 'seq'), may hold values from -0.078125 to 0.078125
- prefix_key_cache: bfloat16 [16, 12288, 1024], P('tensor', 'seq'), may hold values from -140 to 140
- prefix_value_cache: bfloat16 [16, 12288, 1024], P('tensor', 'seq'), may hold values from -6 to 6
- suffix_key_cache: bfloat16 [64, 4096, 1024], P('tensor', 'seq'), may hold values from -8 to 8
- suffix_value_cache: bfloat16 [64, 4096, 1024], P('tensor', 'seq'), may hold values from -6 to 6
- prefix_lens: int32 [16], P('tensor'), may hold values from 1 to 12288, as said below
- suffix_lens: int32 [64], P('tensor'), may hold values from 0 to 4096, as said below
Outputs:
- attn_out: float32 [4, 64, 5120], P(None, 'tensor', 'seq')
- new_keys: float32 [64, 4, 1024], P('tensor')
- new_values: float32 [64, 4, 1024], P('tensor')
Inputs may be any that keep to these rules, and one draw needn't show every extreme that they name: `prefix_lens`: some group has exactly 12288 live slots and some exactly one. `suffix_lens`: some request has exactly 4096 live slots and some none.
All inputs are finite; a program needn't handle non-finite values.
Results may differ from a plain program's by a relative error of at most 0.012.
The roundings to bfloat16 on the way count: a program that leaves them out, or rounds other values in their place, can miss the bound.
Values may be sent and summed in bfloat16 or wider, within the bound.
No kernel may reach another device: no remote copies, remote signals or barrier semaphores. Data moves between devices by JAX's collectives and lax.ppermute only.
A program may use at most 64 MiB of HBM per device.

v0:
```python
import jax
import jax.numpy as jnp
from jax import lax
from jax.sharding import PartitionSpec as P

D = 5120
QUERY_HEADS = 40
KEY_HEADS = 8
HEAD_SIZE = 128
KEY_COLUMNS = 1024
epsilon = 1e-06
masked_fill = -1e30


def apply_rotary(values, token_positions):
    half = values.shape[-1] // 2
    freq = jnp.exp(
        -(jnp.arange(half, dtype=jnp.float32) * (2.0 / values.shape[-1]))
        * jnp.log(jnp.float32(1000000.0))
    )
    angles = token_positions[..., None, None] * freq
    cosine = jnp.cos(angles)
    sine = jnp.sin(angles)
    left = values[..., :half]
    right = values[..., half:]
    return jnp.concatenate([left * cosine - right * sine, right * cosine + left * sine], axis=-1)


def body(
    hidden,
    norm_gain,
    w_qkv,
    b_qkv,
    w_out,
    prefix_key_cache,
    prefix_value_cache,
    suffix_key_cache,
    suffix_value_cache,
    prefix_lens,
    suffix_lens,
):
    decode_step_count = hidden.shape[0]
    request_count = suffix_lens.shape[0]
    prefix_count = prefix_key_cache.shape[1]
    suffix_count = suffix_key_cache.shape[1]
    query_group_width = QUERY_HEADS // KEY_HEADS
    query_width = QUERY_HEADS * HEAD_SIZE
    query_rows = decode_step_count * query_group_width
    scale = float(HEAD_SIZE) ** (-0.5)
    seq_index = lax.axis_index("seq")
    xf = hidden.astype(jnp.float32)
    squares = lax.psum(jnp.sum(xf * xf, axis=2), "seq")
    normed = (
        xf * lax.rsqrt(squares / D + epsilon)[..., None] * norm_gain.astype(jnp.float32)
    ).astype(jnp.bfloat16)
    partial_value = jnp.einsum("sbd,dc->sbc", normed, w_qkv, preferred_element_type=jnp.float32)
    bias = b_qkv.astype(jnp.float32)
    summed_cols = lax.psum(partial_value, "seq") + bias
    combined_output = lax.all_to_all(summed_cols, "tensor", split_axis=1, concat_axis=2, tiled=True)
    token_positions = (
        (prefix_lens[0] + suffix_lens)[None, :]
        + jnp.arange(decode_step_count, dtype=jnp.int32)[:, None]
    ).astype(jnp.float32)
    query_matrix = apply_rotary(
        combined_output[..., :query_width].reshape(
            decode_step_count, request_count, QUERY_HEADS, HEAD_SIZE
        ),
        token_positions,
    ).astype(jnp.bfloat16)
    keys_float = apply_rotary(
        combined_output[..., query_width : query_width + KEY_COLUMNS].reshape(
            decode_step_count, request_count, KEY_HEADS, HEAD_SIZE
        ),
        token_positions,
    )
    values_float = combined_output[..., query_width + KEY_COLUMNS :].reshape(
        decode_step_count, request_count, KEY_HEADS, HEAD_SIZE
    )
    current_keys = keys_float.astype(jnp.bfloat16)
    current_values = values_float.astype(jnp.bfloat16)
    new_keys = keys_float.reshape(decode_step_count, request_count, KEY_COLUMNS).transpose(1, 0, 2)
    new_values = values_float.reshape(decode_step_count, request_count, KEY_COLUMNS).transpose(
        1, 0, 2
    )
    query_by_group = (
        query_matrix.reshape(
            decode_step_count, request_count, KEY_HEADS, query_group_width, HEAD_SIZE
        )
        .transpose(1, 2, 0, 3, 4)
        .reshape(request_count, KEY_HEADS, query_rows, HEAD_SIZE)
    )
    prefix_key_block = prefix_key_cache[0].reshape(prefix_count, KEY_HEADS, HEAD_SIZE)
    prefix_value_block = prefix_value_cache[0].reshape(prefix_count, KEY_HEADS, HEAD_SIZE)
    suffix_key_block = suffix_key_cache.reshape(request_count, suffix_count, KEY_HEADS, HEAD_SIZE)
    suffix_value_block = suffix_value_cache.reshape(
        request_count, suffix_count, KEY_HEADS, HEAD_SIZE
    )
    score_pre = (
        jnp.einsum(
            "rhqd,phd->rhqp", query_by_group, prefix_key_block, preferred_element_type=jnp.float32
        )
        * scale
    )
    score_suf = (
        jnp.einsum(
            "rhqd,rshd->rhqs", query_by_group, suffix_key_block, preferred_element_type=jnp.float32
        )
        * scale
    )
    pre_mask = (
        seq_index * prefix_count + jnp.arange(prefix_count, dtype=jnp.int32) < prefix_lens[0]
    )[None, None, None, :]
    suf_mask = (
        (seq_index * suffix_count + jnp.arange(suffix_count, dtype=jnp.int32))[None, :]
        < suffix_lens[:, None]
    )[:, None, None, :]
    fill_pre = jnp.where(pre_mask, score_pre, masked_fill)
    fill_suf = jnp.where(suf_mask, score_suf, masked_fill)
    local_max = jnp.maximum(jnp.max(fill_pre, axis=3), jnp.max(fill_suf, axis=3))
    prob_pre = jnp.where(pre_mask, jnp.exp(fill_pre - local_max[..., None]), 0.0)
    prob_suf = jnp.where(suf_mask, jnp.exp(fill_suf - local_max[..., None]), 0.0)
    local_weight = jnp.sum(prob_pre, axis=3) + jnp.sum(prob_suf, axis=3)
    local_acc = jnp.einsum(
        "rhqp,phd->rhqd",
        prob_pre.astype(jnp.bfloat16),
        prefix_value_block,
        preferred_element_type=jnp.float32,
    )
    local_acc = local_acc + jnp.einsum(
        "rhqs,rshd->rhqd",
        prob_suf.astype(jnp.bfloat16),
        suffix_value_block,
        preferred_element_type=jnp.float32,
    )
    global_max = lax.pmax(local_max, "seq")
    factor = jnp.exp(local_max - global_max)
    global_weight, global_acc = lax.psum(
        (local_weight * factor, local_acc * factor[..., None]), "seq"
    )
    fresh_k = current_keys.transpose(1, 2, 0, 3)
    fresh_v = current_values.transpose(1, 2, 0, 3)
    score_new = (
        jnp.einsum("rhqd,rhid->rhqi", query_by_group, fresh_k, preferred_element_type=jnp.float32)
        * scale
    )
    new_mask = (
        (jnp.arange(query_rows, dtype=jnp.int32) // query_group_width)[:, None]
        >= jnp.arange(decode_step_count, dtype=jnp.int32)[None, :]
    )[None, None]
    fill_new = jnp.where(new_mask, score_new, masked_fill)
    new_max = jnp.max(fill_new, axis=3)
    prob_new = jnp.where(new_mask, jnp.exp(fill_new - new_max[..., None]), 0.0)
    top = jnp.maximum(global_max, new_max)
    factor_old = jnp.exp(global_max - top)
    factor_new = jnp.exp(new_max - top)
    total = global_weight * factor_old + jnp.sum(prob_new, axis=3) * factor_new
    new_acc = jnp.einsum(
        "rhqi,rhid->rhqd",
        prob_new.astype(jnp.bfloat16),
        fresh_v,
        preferred_element_type=jnp.float32,
    )
    summed = global_acc * factor_old[..., None] + new_acc * factor_new[..., None]
    attention_output = (summed / total[..., None]).astype(jnp.bfloat16)
    heads_local = (
        attention_output.reshape(
            request_count, KEY_HEADS, decode_step_count, query_group_width, HEAD_SIZE
        )
        .transpose(2, 0, 1, 3, 4)
        .reshape(decode_step_count, request_count, query_width)
    )
    by_heads = lax.all_to_all(heads_local, "tensor", split_axis=2, concat_axis=1, tiled=True)
    projected = jnp.einsum("sbc,cd->sbd", by_heads, w_out, preferred_element_type=jnp.float32)
    owned = lax.psum_scatter(projected, "tensor", scatter_dimension=1, tiled=True)
    return (owned, new_keys, new_values)


def solution(mesh):
    placed = (
        P(None, None, "seq"),
        P("seq"),
        P("seq", "tensor"),
        P("tensor"),
        P("tensor", "seq"),
        P("tensor", "seq", None),
        P("tensor", "seq", None),
        P("tensor", "seq", None),
        P("tensor", "seq", None),
        P("tensor"),
        P("tensor"),
    )
    return jax.shard_map(
        body,
        mesh=mesh,
        in_specs=placed,
        out_specs=(P(None, "tensor", "seq"), P("tensor", None, None), P("tensor", None, None)),
        check_vma=False,
    )
```

profile of v0, /device:TPU:2, one launch (start us, length us, event | category | flops | bytes accessed | tf_op | source)
XLA Modules:
  0.0 850.0 jit_solution(4505224170774639408)
XLA Ops:
  7.3 0.8 convert_element_type.43
  8.0 1.0 fusion.22
  9.1 54.7 %psum.28 = f32[4,64]{1,0:T(4,128)S(1)} all-reduce(f32[4,64]{1,0:T(4,128)S(1)} %fusion.22), channel_id=1, replica_groups=mesh['seq'=32,'tensor'=16] {'seq'}, use_global_device_ids=true, to_apply=%region_1.0 | all-reduce | flops 256 | bytes 2048 | tf_op jit(solution)/shard_map/psum | solution.py:52
  63.8 2.1 fusion.29
  66.6 0.1 add_convert_fusion.1
  66.6 0.1 multiply_cosine_fusion
  66.9 0.2 copy.148
  67.1 2.2 copy.149
  69.3 199.9 %all-reduce.5.cloned.1.call-done = f32[4,64,448]{2,1,0:T(8,128)} async-done(((f32[4,64,448]{2,1,0:T(8,128)}), f32[4,64,448]{2,1,0:T(8,128)}) %all-reduce.5.cloned.1.call-update) | async-done | bytes 458768 | tf_op jit(solution)/shard_map/psum | solution.py:58
  269.2 1.1 broadcast_add_fusion
  270.4 1.1 copy.98
  271.5 7.3 all-to-all-start
  278.8 0.5 iota_compare_fusion
  279.4 0.1 broadcast_compare_fusion
  279.4 9.8 %all-to-all-done = f32[4,64,448]{2,0,1:T(4,128)S(1)} async-done(((f32[4,64,448]{2,0,1:T(4,128)}), f32[4,64,448]{2,0,1:T(4,128)S(1)}, u32[]{:S(2)}, u32[]{:S(2)}) %all-to-all-start) | async-done | bytes 458784 | tf_op jit(solution)/shard_map/all_to_all | solution.py:59
  289.2 0.3 copy.99
  289.5 0.3 all_to_all.29
  289.9 0.6 slice_bitcast_fusion.1
  290.6 0.1 reshape.150
  290.7 0.2 fusion.51
  290.9 0.4 subtract_convert_fusion
  291.3 0.2 maximum_bitcast_fusion
  291.6 1.4 fusion.52
  293.0 0.7 fusion.53
  293.7 91.2 %pmax.7 = f32[4,8,20]{2,1,0:T(8,128)} all-reduce(f32[4,8,20]{2,1,0:T(8,128)S(1)} %copy_maximum_fusion), channel_id=1, replica_groups=mesh['seq'=32,'tensor'=16] {'seq'}, use_global_device_ids=true, to_apply=%region_5.6 | all-reduce | flops 640 | bytes 5120 | tf_op jit(solution)/shard_map/pmax | solution.py:135
  384.9 1.5 multiply_subtract_fusion
  386.4 1.9 fusion.20
  388.2 1.1 fusion.12
  389.3 90.0 %psum.31 = f32[4,8,20]{2,1,0:T(8,128)S(1)} all-reduce(f32[4,8,20]{2,1,0:T(8,128)S(1)} %get-tuple-element.6), channel_id=1, replica_groups=mesh['seq'=32,'tensor'=16] {'seq'}, use_global_device_ids=true, to_apply=%region_10.11 | all-reduce | flops 640 | bytes 5120 | tf_op jit(solution)/shard_map/psum | solution.py:137
  479.4 1.3 convolution_bitcast_fusion
  480.8 1.2 fusion.4
  482.0 0.3 fusion.54
  482.3 0.1 fusion.37
  482.5 198.4 %all-reduce.7.cloned.1.call-done = f32[4,8,20,128]{3,2,0,1:T(8,128)} async-done(((f32[4,8,20,128]{3,2,0,1:T(8,128)}), f32[4,8,20,128]{3,2,0,1:T(8,128)}) %all-reduce.7.cloned.1.call-update) | async-done | bytes 327696 | tf_op jit(solution)/shard_map/psum | solution.py:137
  680.9 1.5 fusion.6
  682.3 0.1 copy.121
  682.4 4.5 copy.139
  686.9 11.0 %reshape.165 = bf16[16,2,2560]{2,1,0:T(2,128)(2,1)S(1)} reshape(bf16[5120,4,4]{2,1,0:T(4,128)(2,1)} %bitcast.84) | data formatting | bytes 327680
  697.9 13.9 %all_to_all.36 = bf16[16,2,2560]{2,1,0:T(2,128)(2,1)S(1)} all-to-all(bf16[16,2,2560]{2,1,0:T(2,128)(2,1)S(1)} %reshape.165), channel_id=1, replica_groups=mesh['seq'=32,'tensor'=16] {'tensor'}, dimensions={0} | all-to-all | bytes 327680 | tf_op jit(solution)/shard_map/all_to_all | solution.py:172
  711.8 12.3 %reshape.166 = bf16[5120,4,4]{2,1,0:T(4,128)(2,1)} reshape(bf16[16,2,2560]{2,1,0:T(2,128)(2,1)S(1)} %all_to_all.36) | data formatting | bytes 327680
  724.1 6.4 copy.140
  730.5 0.1 copy.125
  730.6 0.1 all_to_all.33
  730.7 0.9 fusion.34
  731.7 1.3 dynamic-slice
  733.6 0.7 fusion.46
  734.4 107.7 %all-reduce.9.cloned.1.call-done = f32[4,64,160]{2,1,0:T(8,128)} async-done(((f32[4,64,160]{2,1,0:T(8,128)}), f32[4,64,160]{2,1,0:T(8,128)}) %all-reduce.9.cloned.1.call-update) | async-done | bytes 163856
  842.1 1.4 constant_dynamic-slice_fusion
  (65 shorter events, 0.4 us)
Async XLA Ops:
  7.2 284.4 %copy-start = (bf16[4,128,1024]{2,1,0:T(8,128)(2,1)S(1)}, bf16[4,128,1024]{2,1,0:T(8,128)(2,1)}, u32[]{:S(2)}) copy-start(bf16[4,128,1024]{2,1,0:T(8,128)(2,1)} %param.18) | copy-start | bytes 3145732
  7.2 59.4 %copy-start.19 = (s32[4]{0:T(128)S(1)}, s32[4]{0:T(128)}, u32[]{:S(2)}) copy-start(s32[4]{0:T(128)} %param.21) | copy-start | bytes 52
  7.2 59.6 %copy-start.16 = (bf16[448]{0:T(512)(128)(2,1)S(1)}, bf16[448]{0:T(512)(128)(2,1)}, u32[]{:S(2)}) copy-start(bf16[448]{0:T(512)(128)(2,1)} %param.14) | copy-start | bytes 2692
  7.2 59.7 %copy-start.4 = (bf16[1,384,1024]{2,1,0:T(8,128)(2,1)S(1)}, bf16[1,384,1024]{2,1,0:T(8,128)(2,1)}, u32[]{:S(2)}) copy-start(bf16[1,384,1024]{2,1,0:T(8,128)(2,1)} %param.16) | copy-start | bytes 2359300
  7.2 262.0 %all-reduce.5.cloned.1.call-start = ((), (), s32[]{:S(2)}) async-start(), calls=%async_computation.2 | async-start | bytes 1048576 | tf_op jit(solution)/shard_map/psum | solution.py:58
  66.8 2.5 copy-start.12
  66.8 2.5 copy-start.13
  69.3 223.7 %copy-start.15 = (pred[384]{0:T(512)(128)(4,1)}, pred[384]{0:T(512)(128)(4,1)S(1)}, u32[]{:S(2)}) copy-start(pred[384]{0:T(512)(128)(4,1)S(1)} %add_compare_fusion) | copy-start | bytes 1156
  271.5 17.7 %all-to-all-start = ((f32[4,64,448]{2,0,1:T(4,128)}), f32[4,64,448]{2,0,1:T(4,128)S(1)}, u32[]{:S(2)}, u32[]{:S(2)}) async-start(f32[4,64,448]{2,0,1:T(4,128)} %copy.98), calls=%async_computation | async-start | bytes 1048576 | tf_op jit(solution)/shard_map/all_to_all | solution.py:59
  278.8 402.1 %all-reduce.7.cloned.1.call-start = ((), (), s32[]{:S(2)}) async-start(), calls=%async_computation.3 | async-start | bytes 786432 | tf_op jit(solution)/shard_map/psum | solution.py:137
  279.4 12.2 %copy-start.18 = (pred[4,128]{1,0:T(4,128)(4,1)}, pred[4,128]{1,0:T(4,128)(4,1)S(1)}, u32[]{:S(2)}) copy-start(pred[4,128]{1,0:T(4,128)(4,1)S(1)} %broadcast_compare_fusion) | copy-start | bytes 1540
  291.6 2.1 copy-start.2
  293.7 185.6 %copy-start.5 = (bf16[48,8,8,128]{3,2,1,0:T(8,128)(2,1)S(1)}, bf16[48,8,8,128]{3,2,1,0:T(8,128)(2,1)}, u32[]{:S(2)}) copy-start(bf16[48,8,8,128]{3,2,1,0:T(8,128)(2,1)} %copy.149) | copy-start | bytes 2359300
  384.9 4.4 copy-start.9
  384.9 4.4 copy-start.14
  479.4 1.3 copy-start.1
  479.4 1.3 copy-start.6
  480.7 1.3 copy-start.3
  480.7 1.3 copy-start.7
  480.7 1.3 copy-start.8
  480.7 1.3 copy-start.17
  480.7 1.7 copy-start.10
  481.9 360.1 %all-reduce.9.cloned.1.call-start = ((), (), s32[]{:S(2)}) async-start(), calls=%async_computation.4 | async-start | bytes 524288
  724.1 6.6 copy-start.11
Sparse Core Ops, SparseCore 0:
  66.0 203.1 all-reduce.4
  482.1 198.7 all-reduce.6
  731.8 110.2 all-reduce.8
where the time goes:
time: 851 us; the launch traced here: 850 us
  waiting for transfers between devices  516 us (61%)
  blocking collectives  250 us (29%)
  local copies, waits for them, and re-layouts  42.4 us (5%)
  between operations  15.5 us (2%)
  other arithmetic  9.67 us (1%)
  matrix products  9.33 us (1%)
    psum x1, waiting for transfers between devices, body(): summed_cols = lax.psum(partial_value, 'seq') + bias  200 us
    psum x1, waiting for transfers between devices, body(): lax.psum((local_weight * factor, local_acc * factor[..., None]), 'seq')  198 us
    unnamed x4, waiting for transfers between devices  108 us
    pmax x1, blocking collectives, body(): global_max = lax.pmax(local_max, 'seq')  91.2 us
    psum x1, blocking collectives, body(): lax.psum((local_weight * factor, local_acc * factor[..., None]), 'seq')  90 us
    psum x1, blocking collectives, body(): squares = lax.psum(jnp.sum(xf * xf, axis=2), 'seq')  54.7 us
    unnamed x46, local copies, waits for them, and re-layouts  28.4 us
  transfers between devices with their start and end apart: 4, of which 4 were waited for; matrix products, arithmetic and copies ran while one was open for 1% of the time, Pallas kernels for 0%

commit v1 on v0

--- a/solution.py
+++ b/solution.py
@@ -55,7 +55,7 @@
     ).astype(jnp.bfloat16)
     partial_value = jnp.einsum("sbd,dc->sbc", normed, w_qkv, preferred_element_type=jnp.float32)
     bias = b_qkv.astype(jnp.float32)
-    summed_cols = lax.psum(partial_value, "seq") + bias
+    summed_cols = jnp.sum(lax.all_gather(partial_value, "seq"), axis=0) + bias
     combined_output = lax.all_to_all(summed_cols, "tensor", split_axis=1, concat_axis=2, tiled=True)
     token_positions = (
         (prefix_lens[0] + suffix_lens)[None, :]

time: 851 us -> 754 us (0.89)
  waiting for transfers between devices: 516 us -> 413 us
    psum x1 -> x0, waiting for transfers between devices: 200 us -> none  [body(): summed_cols = lax.psum(partial_value, 'seq') + bias]
    all_gather x0 -> x1, waiting for transfers between devices: none -> 98.5 us  [body(): summed_cols = jnp.sum(lax.all_gather(partial_value, 'seq'), axis=0) + bias]
    unnamed x46 -> x49, local copies, waits for them, and re-layouts: 28.4 us -> 29.7 us
where the time goes in v1:
time: 754 us; the launch traced here: 753 us
  waiting for transfers between devices  413 us (55%)
  blocking collectives  249 us (33%)
  local copies, waits for them, and re-layouts  44.7 us (6%)
  between operations  15.5 us (2%)
  other arithmetic  14.5 us (2%)
  matrix products  9.21 us (1%)
  starting transfers between devices  7.57 us (1%)
    psum x1, waiting for transfers between devices, body(): lax.psum((local_weight * factor, local_acc * factor[..., None]), 'seq')  198 us
    unnamed x4, waiting for transfers between devices  107 us
    all_gather x1, waiting for transfers between devices, body(): summed_cols = jnp.sum(lax.all_gather(partial_value, 'seq'), axis=0) + bias  98.5 us
    psum x1, blocking collectives, body(): lax.psum((local_weight * factor, local_acc * factor[..., None]), 'seq')  90 us
    pmax x1, blocking collectives, body(): global_max = lax.pmax(local_max, 'seq')  90 us
    psum x1, blocking collectives, body(): squares = lax.psum(jnp.sum(xf * xf, axis=2), 'seq')  54.7 us
    unnamed x49, local copies, waits for them, and re-layouts  29.7 us
  transfers between devices with their start and end apart: 4, of which 4 were waited for; matrix products, arithmetic and copies ran while one was open for 1% of the time, Pallas kernels for 0%

profile of v1, /device:TPU:2, one launch (start us, length us, event | category | flops | bytes accessed | tf_op | source)
XLA Modules:
  0.0 753.4 jit_solution(4849049653169618925)
XLA Ops:
  7.3 1.1 fusion.22
  8.4 54.7 %psum.21 = f32[4,64]{1,0:T(4,128)S(1)} all-reduce(f32[4,64]{1,0:T(4,128)S(1)} %fusion.22), channel_id=1, replica_groups=mesh['seq'=32,'tensor'=16] {'seq'}, use_global_device_ids=true, to_apply=%region_1.0 | all-reduce | flops 256 | bytes 2048 | tf_op jit(solution)/shard_map/psum | solution.py:52
  63.1 0.7 convert_element_type.43
  63.8 2.0 fusion.29
  66.6 0.1 multiply_cosine_fusion
  66.8 0.6 copy-done.11
  67.4 0.2 copy.204
  67.6 2.2 copy.205
  69.9 98.5 %all-gather.3.cloned.1.call-done = f32[128,64,448]{2,1,0:T(8,128)} async-done(((f32[4,64,448]{2,1,0:T(8,128)}), f32[128,64,448]{2,1,0:T(8,128)}) %all-gather.3.cloned.1.call-update) | async-done | bytes 14680080 | tf_op jit(solution)/shard_map/all_gather | solution.py:58
  168.3 7.8 %reduce_sum.46 = f32[4,64,448]{2,1,0:T(8,128)S(1)} reduce(f32[32,4,64,448]{3,2,1,0:T(8,128)} %bitcast.82, f32[]{:T(128)} %constant.9.clone.1), dimensions={0}, to_apply=%region_2.0 | reduce | flops 3555328 | bytes 15138820 | tf_op jit(solution)/shard_map/reduce_sum | solution.py:58
  176.2 1.1 copy.149
  177.3 7.3 all-to-all-start
  184.7 0.6 iota_compare_fusion
  185.3 9.9 %all-to-all-done = f32[4,64,448]{2,0,1:T(4,128)S(1)} async-done(((f32[4,64,448]{2,0,1:T(4,128)}), f32[4,64,448]{2,0,1:T(4,128)S(1)}, u32[]{:S(2)}, u32[]{:S(2)}) %all-to-all-start) | async-done | bytes 458784 | tf_op jit(solution)/shard_map/all_to_all | solution.py:59
  195.2 0.3 copy.150
  195.5 0.3 all_to_all.29
  195.9 0.3 subtract_convert_fusion
  196.2 0.2 maximum_bitcast_fusion
  196.5 0.7 fusion.53
  197.1 1.4 fusion.52
  198.6 0.6 copy.161
  199.2 90.0 %pmax.7 = f32[4,8,20]{2,1,0:T(8,128)} all-reduce(f32[4,8,20]{2,1,0:T(8,128)S(1)} %copy_maximum_fusion), channel_id=1, replica_groups=mesh['seq'=32,'tensor'=16] {'seq'}, use_global_device_ids=true, to_apply=%region_5.6 | all-reduce | flops 640 | bytes 5120 | tf_op jit(solution)/shard_map/pmax | solution.py:135
  289.2 0.6 slice_bitcast_fusion.1
  289.8 0.6 slice.42
  290.5 1.4 fusion.20
  291.9 1.1 fusion.12
  293.0 90.0 %psum.23 = f32[4,8,20]{2,1,0:T(8,128)S(1)} all-reduce(f32[4,8,20]{2,1,0:T(8,128)S(1)} %get-tuple-element.21), channel_id=1, replica_groups=mesh['seq'=32,'tensor'=16] {'seq'}, use_global_device_ids=true, to_apply=%region_10.11 | all-reduce | flops 640 | bytes 5120 | tf_op jit(solution)/shard_map/psum | solution.py:137
  383.1 0.1 fusion.51
  383.2 1.2 convolution_bitcast_fusion
  384.5 1.2 fusion.4
  385.7 0.2 all-reduce.6.cloned.1.call-start
  385.9 0.1 multiply_subtract_fusion
  386.0 0.3 fusion.54
  386.5 197.8 %all-reduce.4.cloned.1.call-done = f32[4,8,20,128]{3,2,0,1:T(8,128)} async-done(((f32[4,8,20,128]{3,2,0,1:T(8,128)}), f32[4,8,20,128]{3,2,0,1:T(8,128)}) %all-reduce.4.cloned.1.call-update) | async-done | bytes 327696 | tf_op jit(solution)/shard_map/psum | solution.py:137
  584.3 1.5 fusion.6
  585.9 4.5 copy.195
  590.4 11.0 %reshape.166 = bf16[16,2,2560]{2,1,0:T(2,128)(2,1)S(1)} reshape(bf16[5120,4,4]{2,1,0:T(4,128)(2,1)} %bitcast.80) | data formatting | bytes 327680
  601.3 13.9 %all_to_all.36 = bf16[16,2,2560]{2,1,0:T(2,128)(2,1)S(1)} all-to-all(bf16[16,2,2560]{2,1,0:T(2,128)(2,1)S(1)} %reshape.166), channel_id=1, replica_groups=mesh['seq'=32,'tensor'=16] {'tensor'}, dimensions={0} | all-to-all | bytes 327680 | tf_op jit(solution)/shard_map/all_to_all | solution.py:172
  615.2 12.3 %reshape.167 = bf16[5120,4,4]{2,1,0:T(4,128)(2,1)} reshape(bf16[16,2,2560]{2,1,0:T(2,128)(2,1)S(1)} %all_to_all.36) | data formatting | bytes 327680
  627.5 6.4 copy.196
  634.0 0.1 copy.179
  634.1 0.1 all_to_all.33
  634.2 0.9 fusion.34
  635.1 1.3 dynamic-slice
  637.1 0.7 copy.180
  637.7 0.7 fusion.46
  638.5 107.0 %all-reduce.6.cloned.1.call-done = f32[4,64,160]{2,1,0:T(8,128)} async-done(((f32[4,64,160]{2,1,0:T(8,128)}), f32[4,64,160]{2,1,0:T(8,128)}) %all-reduce.6.cloned.1.call-update) | async-done | bytes 163856
  745.5 1.4 constant_dynamic-slice_fusion
  (71 shorter events, 0.8 us)
Async XLA Ops:
  7.2 190.0 %copy-start = (bf16[4,128,1024]{2,1,0:T(8,128)(2,1)S(1)}, bf16[4,128,1024]{2,1,0:T(8,128)(2,1)}, u32[]{:S(2)}) copy-start(bf16[4,128,1024]{2,1,0:T(8,128)(2,1)} %param.18) | copy-start | bytes 3145732
  7.2 59.3 %copy-start.20 = (s32[4]{0:T(128)S(1)}, s32[4]{0:T(128)}, u32[]{:S(2)}) copy-start(s32[4]{0:T(128)} %param.21) | copy-start | bytes 52
  7.2 60.2 %copy-start.17 = (bf16[448]{0:T(512)(128)(2,1)S(1)}, bf16[448]{0:T(512)(128)(2,1)}, u32[]{:S(2)}) copy-start(bf16[448]{0:T(512)(128)(2,1)} %param.14) | copy-start | bytes 2692
  7.2 60.2 %copy-start.4 = (bf16[1,384,1024]{2,1,0:T(8,128)(2,1)S(1)}, bf16[1,384,1024]{2,1,0:T(8,128)(2,1)}, u32[]{:S(2)}) copy-start(bf16[1,384,1024]{2,1,0:T(8,128)(2,1)} %param.16) | copy-start | bytes 2359300
  7.2 161.1 %all-gather.3.cloned.1.call-start = ((), (), s32[]{:S(2)}) async-start(), calls=%async_computation.3 | async-start | bytes 17301504 | tf_op jit(solution)/shard_map/all_gather | solution.py:58
  66.8 0.6 copy-start.11
  66.8 0.6 copy-start.13
  69.9 126.6 %copy-start.16 = (pred[384]{0:T(512)(128)(4,1)}, pred[384]{0:T(512)(128)(4,1)S(1)}, u32[]{:S(2)}) copy-start(pred[384]{0:T(512)(128)(4,1)S(1)} %add_compare_fusion) | copy-start | bytes 1156
  177.3 17.9 %all-to-all-start = ((f32[4,64,448]{2,0,1:T(4,128)}), f32[4,64,448]{2,0,1:T(4,128)S(1)}, u32[]{:S(2)}, u32[]{:S(2)}) async-start(f32[4,64,448]{2,0,1:T(4,128)} %copy.149), calls=%async_computation | async-start | bytes 1048576 | tf_op jit(solution)/shard_map/all_to_all | solution.py:59
  184.6 399.7 %all-reduce.4.cloned.1.call-start = ((), (), s32[]{:S(2)}) async-start(), calls=%async_computation.2 | async-start | bytes 786432 | tf_op jit(solution)/shard_map/psum | solution.py:137
  185.3 11.8 %copy-start.19 = (pred[4,128]{1,0:T(4,128)(4,1)}, pred[4,128]{1,0:T(4,128)(4,1)S(1)}, u32[]{:S(2)}) copy-start(pred[4,128]{1,0:T(4,128)(4,1)S(1)} %broadcast_compare_fusion) | copy-start | bytes 1540
  196.4 2.1 copy-start.2
  289.2 3.8 copy-start.7
  290.4 92.6 %copy-start.6 = (f32[4,4,1024]{2,1,0:T(4,128)S(1)}, f32[4,4,1024]{2,1,0:T(4,128)}, u32[]{:S(2)}) copy-start(f32[4,4,1024]{2,1,0:T(4,128)} %get-tuple-element.24) | copy-start | bytes 196612
  290.4 92.7 %copy-start.5 = (bf16[48,8,8,128]{3,2,1,0:T(8,128)(2,1)S(1)}, bf16[48,8,8,128]{3,2,1,0:T(8,128)(2,1)}, u32[]{:S(2)}) copy-start(bf16[48,8,8,128]{3,2,1,0:T(8,128)(2,1)} %copy.205) | copy-start | bytes 2359300
  290.5 92.7 %copy-start.15 = (f32[4,8,20]{2,0,1:T(4,128)S(1)}, f32[4,8,20]{2,0,1:T(4,128)}, u32[]{:S(2)}) copy-start(f32[4,8,20]{2,0,1:T(4,128)} %copy.161) | copy-start | bytes 7684
  383.2 1.3 copy-start.1
  384.4 1.5 copy-start.12
  384.4 1.5 copy-start.14
  384.5 1.6 copy-start.3
  384.5 1.6 copy-start.18
  384.5 1.9 copy-start.8
  385.6 0.8 copy-start.9
  385.7 359.8 %all-reduce.6.cloned.1.call-start = ((), (), s32[]{:S(2)}) async-start(), calls=%async_computation.4 | async-start | bytes 524288
  627.5 6.6 copy-start.10
Sparse Core Ops, SparseCore 0:
  66.0 102.3 all-gather.2
  385.8 198.4 all-reduce.3
  635.3 110.1 all-reduce.5
